TPU v7x, 32 devices: a whole 2x2x4 slice. The times are simulated.
32 devices in a mesh: groups: 2 (over x), blk: 16 (over z, y, core).
Axes of the slice: x: 2, y: 2, z: 4, core: 2. Of those that a mesh axis runs over, the one named last changes fastest.
Arguments:
- paths: bfloat16 [4096, 512], P(('groups', 'blk')), parts along dimension 0, may hold values from -6 to 6
- deltas: bfloat16 [4096, 512], P(('groups', 'blk')), parts along dimension 0, may hold values from -6 to 6
- payoffs: bfloat16 [4096], P(('groups', 'blk')), parts along dimension 0, may hold values from -6 to 6
- counts: int32 [32, 16], P('groups'), parts along dimension 0, may hold values from 0 to 8, as said below
- w_first: bfloat16 [1024, 1024], P(('groups', 'blk')), parts along dimension 0, may hold values from -0.25 to 0.25
- w_second: bfloat16 [2048, 1024], P(('groups', 'blk')), parts along dimension 0, may hold values from -0.1875 to 0.1875
- w_out: bfloat16 [2048], P('groups'), parts along dimension 0, may hold values from -0.1875 to 0.1875
- mom_first: float32 [1024, 1024], P(('groups', 'blk')), parts along dimension 0, may hold values from -6 to 6
- mom_second: float32 [2048, 1024], P(('groups', 'blk')), parts along dimension 0, may hold values from -6 to 6
- mom_out: float32 [2048], P('groups'), parts along dimension 0, may hold values from -6 to 6
Outputs:
- new_first: float32 [1024, 1024], P(('groups', 'blk')), parts along dimension 0
- new_second: float32 [2048, 1024], P(('groups', 'blk')), parts along dimension 0
- new_out: float32 [2048], P('groups'), parts along dimension 0
There are 2 independent parts, one for each index of `groups`. A program takes and returns all parts, laid end to end along the dimension named above; each array names one. Nothing has to cross between parts.
Inputs may be any that keep to these rules, and one draw needn't show every extreme that they name: Source s hands its valid paths, slot 0 onward, to the trainers in order: counts[s, d] of them to trainer d. Every trainer receives 64 paths or fewer in all, and one receives exactly 64; one source hands 8 to every trainer.
All inputs are finite; a program needn't handle non-finite values.
Results may differ from a plain program's by a relative error of at most 0.00035.
The roundings to bfloat16 on the way count: a program that leaves them out, or rounds other values in their place, can miss the bound.
Values may be sent and summed in bfloat16 or wider, within the bound.
No kernel may reach another device: no remote copies, remote signals or barrier semaphores. Data moves between devices by JAX's collectives and lax.ppermute only.
A program may use at most 64 MiB of HBM per device.

v0:
```python
import jax
import jax.numpy as jnp
from jax import lax
from jax.sharding import PartitionSpec as P


def rows_product(left, right):
    return lax.dot_general(
        left, right, (((0,), (0,)), ((), ())), preferred_element_type=jnp.float32
    )


def twin_terms(x_rows, z_rows, y_rows, mask, w_one, w_two, w_three):
    w_outf = w_three.astype(jnp.float32)
    a_one = jnp.dot(x_rows, w_one, preferred_element_type=jnp.float32)
    s_one = jax.nn.sigmoid(a_one)
    h_one = jax.nn.softplus(a_one).astype(jnp.bfloat16)
    a_two = jnp.dot(h_one, w_two, preferred_element_type=jnp.float32)
    s_two = jax.nn.sigmoid(a_two)
    h_two = jax.nn.softplus(a_two)
    value = jnp.sum(h_two * w_outf[None, :], axis=1)
    g_two = (s_two * w_outf[None, :]).astype(jnp.bfloat16)
    c_one = lax.dot_general(
        g_two, w_two, (((1,), (1,)), ((), ())), preferred_element_type=jnp.float32
    )
    g_one = (c_one * s_one).astype(jnp.bfloat16)
    slope = lax.dot_general(
        g_one, w_one, (((1,), (1,)), ((), ())), preferred_element_type=jnp.float32
    )
    e_value = 2.0 * mask * (value - y_rows.astype(jnp.float32))
    e_slope = (2.0 * mask[:, None] * (slope - z_rows.astype(jnp.float32))).astype(jnp.bfloat16)
    e_gone = jnp.dot(e_slope, w_one, preferred_element_type=jnp.float32)
    e_cone = (e_gone * s_one).astype(jnp.bfloat16)
    e_sone = e_gone * c_one
    e_gtwo = jnp.dot(e_cone, w_two, preferred_element_type=jnp.float32)
    grad_three = jnp.sum(e_gtwo * s_two + e_value[:, None] * h_two, axis=0)
    e_atwo = (
        e_gtwo * w_outf[None, :] * s_two * (1.0 - s_two)
        + e_value[:, None] * w_outf[None, :] * s_two
    ).astype(jnp.bfloat16)
    e_hone = lax.dot_general(
        e_atwo, w_two, (((1,), (1,)), ((), ())), preferred_element_type=jnp.float32
    )
    e_aone = (e_sone * s_one * (1.0 - s_one) + e_hone * s_one).astype(jnp.bfloat16)
    return (e_slope, g_one, e_aone, e_cone, g_two, h_one, e_atwo, grad_three)


def normalized(grad):
    return grad / jnp.sqrt(jnp.mean(grad * grad, axis=-1, keepdims=True) + 1e-06)


def per_device(
    paths, deltas, payoffs, counts, w_first, w_second, w_out, mom_first, mom_second, mom_out
):
    position = lax.axis_index("blk")
    rows_dev = paths.shape[0]
    w_one, w_two = (
        lax.all_gather(w_first, "blk", axis=0, tiled=True),
        lax.all_gather(w_second, "blk", axis=0, tiled=True),
    )
    sending = lax.dynamic_index_in_dim(counts, position, 0, keepdims=False)
    x_rows, z_rows, y_rows = (paths, deltas, payoffs)
    total = jnp.sum(sending)
    mask = (jnp.arange(rows_dev, dtype=jnp.int32) < total).astype(jnp.float32)
    e_slope, g_one, e_aone, e_cone, g_two, h_one, e_atwo, grad_three = twin_terms(
        x_rows, z_rows, y_rows, mask, w_one, w_two, w_out
    )
    grad_one = lax.psum_scatter(
        rows_product(x_rows, e_aone) + rows_product(e_slope, g_one),
        "blk",
        scatter_dimension=0,
        tiled=True,
    )
    grad_two = lax.psum_scatter(
        rows_product(e_cone, g_two) + rows_product(h_one, e_atwo),
        "blk",
        scatter_dimension=0,
        tiled=True,
    )
    grad_out = lax.psum(grad_three, "blk")
    new_first = 0.8 * mom_first + 0.2 * normalized(grad_one)
    new_second = 0.8 * mom_second + 0.2 * normalized(grad_two)
    new_out = 0.8 * mom_out + 0.2 * normalized(grad_out)
    return (new_first, new_second, new_out)


def solution(mesh):
    in_specs = (
        P(("groups", "blk"), None),
        P(("groups", "blk"), None),
        P(("groups", "blk")),
        P("groups", None),
        P(("groups", "blk"), None),
        P(("groups", "blk"), None),
        P("groups"),
        P(("groups", "blk"), None),
        P(("groups", "blk"), None),
        P("groups"),
    )
    out_specs = (P(("groups", "blk"), None), P(("groups", "blk"), None), P("groups"))
    return jax.shard_map(
        per_device, mesh=mesh, in_specs=in_specs, out_specs=out_specs, check_vma=False
    )
```

profile of v0, /device:TPU:0, one launch (start us, length us, event | category | flops | bytes accessed | tf_op | source)
XLA Modules:
  0.0 254.4 jit_solution(2150444523015975469)
XLA Ops:
  7.2 0.0 copy-start
  7.2 0.0 all-gather.3.cloned.1.call-start
  7.2 0.7 all-gather.3.cloned.1.call-update
  7.9 0.0 all-gather.5.cloned.1.call-start
  8.0 0.7 all-gather.5.cloned.1.call-update
  8.7 0.0 reduce-scatter.7.cloned.1.call-start
  8.7 0.7 convert_element_type.33
  9.4 1.3 dynamic-slice_reduce_fusion
  10.7 0.6 compare_select_fusion.2
  11.4 39.5 %all-gather.3.cloned.1.call-done = bf16[512,1024]{1,0:T(8,128)(2,1)} async-done(((bf16[32,1024]{1,0:T(8,128)(2,1)}), bf16[512,1024]{1,0:T(8,128)(2,1)}) %all-gather.3.cloned.1.call-update) | async-done | bytes 1048592 | tf_op jit(solution)/shard_map/all_gather | solution.py:58
  50.8 0.0 copy-done
  50.9 1.5 fusion.17
  52.4 0.0 copy-start.11
  52.4 41.0 %all-gather.5.cloned.1.call-done = bf16[1024,1024]{1,0:T(8,128)(2,1)} async-done(((bf16[64,1024]{1,0:T(8,128)(2,1)}), bf16[1024,1024]{1,0:T(8,128)(2,1)}) %all-gather.5.cloned.1.call-update) | async-done | bytes 2097168 | tf_op jit(solution)/shard_map/all_gather | solution.py:59
  93.4 0.0 copy-start.2
  93.4 2.6 %multiply_reduce_fusion.1 = (f32[128]{0:T(128)S(1)}, f32[128,1024]{1,0:T(8,128)S(1)}) fusion(f32[1024]{0:T(1024)S(1)} %convert_element_type.33, bf16[1024,1024]{1,0:T(8,128)(2,1)} %all-gather.5.cloned.1.call-done, f32[128,1024]{1,0:T(8,128)S(1)} %fusion.17), kind=kOutput, calls=%fused_computation.16 | convolution fusion | flops 270401408 | bytes 3150336 | tf_op jit(solution)/shard_map/dot_general | solution.py:18
  96.0 0.0 copy-start.3
  96.0 0.0 copy-done.11
  96.0 0.7 subtract_multiply_fusion
  96.7 0.0 copy-done.2
  96.7 0.0 copy-start.1
  96.7 0.0 copy-start.8
  96.7 1.7 multiply_convert_fusion.1
  98.4 0.0 copy-done.1
  98.4 0.0 copy-done.8
  98.4 0.5 fusion.4
  98.9 1.1 multiply_convert_fusion
  100.0 0.0 copy-start.5
  100.0 0.0 copy-done.3
  100.0 0.9 add_reduce_fusion
  100.9 0.0 copy-done.5
  100.9 3.0 %fusion.2 = f32[1024,512]{1,0:T(8,128)S(1)} fusion(bf16[128,512]{1,0:T(8,128)(2,1)S(1)} %copy-done, bf16[128,1024]{1,0:T(8,128)(2,1)S(1)} %get-tuple-element.10, bf16[1024,1024]{1,0:T(8,128)(2,1)} %all-gather.5.cloned.1.call-done, f32[128,1024]{1,0:T(8,128)} %get-tuple-element.14, f32[128,1024]{1,0:T(8,128)} %get-tuple-element.12, f32[128,1024]{1,0:T(8,128)S(1)} %fusion.17), kind=kOutput, calls=%fused_computation.7 | convolution fusion | flops 403963904 | bytes 6160384 | tf_op jit(solution)/shard_map/dot_general | solution.py:8
  103.9 1.8 bitcast_add_fusion
  105.7 2.9 %copy.20 = f32[512,1024]{1,0:T(8,128)} copy(f32[512,1024]{0,1:T(8,128)} %bitcast_add_fusion) | data formatting | bytes 4194304
  108.6 0.0 copy-start.4
  108.6 0.0 copy-start.6
  108.6 0.0 reduce-scatter.7.cloned.1.call-update
  108.7 0.0 reduce-scatter.5.cloned.1.call-start
  108.7 1.0 copy-done.4
  109.7 0.1 copy-done.6
  109.7 0.8 fusion.11
  110.5 2.8 %convolution_add_fusion = f32[1024,1024]{1,0:T(8,128)} fusion(f32[1024,1024]{1,0:T(8,128)S(1)} %fusion.11, bf16[128,1024]{1,0:T(8,128)(2,1)S(1)} %get-tuple-element.10, f32[128,1024]{1,0:T(8,128)S(1)} %fusion.17), kind=kOutput, calls=%fused_computation | convolution fusion | flops 270401536 | bytes 9175040 | tf_op jit(solution)/shard_map/dot_general | solution.py:8
  113.3 0.0 copy-start.9
  113.3 0.0 copy-start.10
  113.3 0.0 reduce-scatter.5.cloned.1.call-update
  113.3 0.9 copy-done.9
  114.2 0.0 copy-start.7
  114.2 0.2 copy.16
  114.4 31.6 %psum.7 = f32[1024]{0:T(1024)S(1)} all-reduce(f32[1024]{0:T(1024)S(1)} %get-tuple-element.9), channel_id=1, replica_groups=mesh['groups'=2,'blk'=16] {'blk'}, use_global_device_ids=true, to_apply=%region_7.8 | all-reduce | flops 1024 | bytes 8192 | tf_op jit(solution)/shard_map/psum | solution.py:80
  146.1 0.6 multiply_reduce_fusion.3
  147.4 0.0 copy-done.10
  147.4 0.6 multiply_add_fusion.2
  148.0 21.5 %reduce-scatter.7.cloned.1.call-done = f32[32,1024]{1,0:T(8,128)} async-done(((f32[512,1024]{1,0:T(8,128)}), f32[32,1024]{1,0:T(8,128)}) %reduce-scatter.7.cloned.1.call-update) | async-done | bytes 131088
  169.5 1.1 copy.21
  170.6 0.2 multiply_reduce_fusion
  170.8 0.1 multiply_add_fusion
  170.9 0.8 copy.18
  171.7 73.3 %reduce-scatter.5.cloned.1.call-done = f32[64,1024]{1,0:T(8,128)} async-done(((f32[1024,1024]{1,0:T(8,128)}), f32[64,1024]{1,0:T(8,128)}) %reduce-scatter.5.cloned.1.call-update) | async-done | bytes 262160 | tf_op jit(solution)/shard_map/reduce_scatter | solution.py:74
  245.0 1.1 multiply_reduce_fusion.2
  246.1 0.0 copy-done.7
  246.1 1.8 multiply_add_fusion.1
  (2 shorter events, 0.0 us)
Async XLA Ops:
  7.2 43.7 %copy-start = (bf16[128,512]{1,0:T(8,128)(2,1)S(1)}, bf16[128,512]{1,0:T(8,128)(2,1)}, u32[]{:S(2)}) copy-start(bf16[128,512]{1,0:T(8,128)(2,1)} %param.10) | copy-start | bytes 393220
  7.2 43.7 %all-gather.3.cloned.1.call-start = ((), (), s32[]{:S(2)}) async-start(), calls=%async_computation.2 | async-start | bytes 1114112 | tf_op jit(solution)/shard_map/all_gather | solution.py:58
  7.9 85.4 %all-gather.5.cloned.1.call-start = ((), (), s32[]{:S(2)}) async-start(), calls=%async_computation.3 | async-start | bytes 2228224 | tf_op jit(solution)/shard_map/all_gather | solution.py:59
  8.7 160.8 %reduce-scatter.7.cloned.1.call-start = ((), (), s32[]{:S(2)}) async-start(), calls=%async_computation.5 | async-start | bytes 2228224
  52.4 43.6 %copy-start.11 = (bf16[128]{0:T(256)(128)(2,1)S(1)}, bf16[128]{0:T(256)(128)(2,1)}, u32[]{:S(2)}) copy-start(bf16[128]{0:T(256)(128)(2,1)} %param.12) | copy-start | bytes 772
  93.4 3.3 %copy-start.2 = (bf16[1024,1024]{1,0:T(8,128)(2,1)S(1)}, bf16[1024,1024]{1,0:T(8,128)(2,1)}, u32[]{:S(2)}) copy-start(bf16[1024,1024]{1,0:T(8,128)(2,1)} %all-gather.5.cloned.1.call-done) | copy-start | bytes 6291460
  96.0 4.0 %copy-start.3 = (f32[128,1024]{1,0:T(8,128)}, f32[128,1024]{1,0:T(8,128)S(1)}, u32[]{:S(2)}) copy-start(f32[128,1024]{1,0:T(8,128)S(1)} %get-tuple-element.16) | copy-start | bytes 1572868
  96.7 1.7 copy-start.1
  96.7 1.7 copy-start.8
  100.0 0.9 copy-start.5
  108.6 1.0 copy-start.4
  108.6 1.1 copy-start.6
  108.7 136.4 %reduce-scatter.5.cloned.1.call-start = ((), (), s32[]{:S(2)}) async-start(), calls=%async_computation.4 | async-start | bytes 4456448 | tf_op jit(solution)/shard_map/reduce_scatter | solution.py:74
  113.3 0.9 copy-start.9
  113.3 34.0 %copy-start.10 = (f32[1024]{0:T(1024)S(1)}, f32[1024]{0:T(1024)}, u32[]{:S(2)}) copy-start(f32[1024]{0:T(1024)} %param.19) | copy-start | bytes 12292
  114.2 131.9 %copy-start.7 = (f32[64,1024]{1,0:T(8,128)S(1)}, f32[64,1024]{1,0:T(8,128)}, u32[]{:S(2)}) copy-start(f32[64,1024]{1,0:T(8,128)} %param.18) | copy-start | bytes 786436
Sparse Core Ops, SparseCore 0:
  10.2 40.6 all-gather.2
  53.0 40.3 all-gather.4
  108.8 60.6 reduce-scatter.6
  173.7 71.2 reduce-scatter.4
where the time goes:
time: 255 us; the launch traced here: 254 us
  waiting for transfers between devices  177 us (69%)
  blocking collectives  31.6 us (12%)
  matrix products  16.7 us (7%)
  between operations  14.6 us (6%)
  other arithmetic  7.63 us (3%)
  local copies, waits for them, and re-layouts  6.99 us (3%)
    reduce_scatter x1, waiting for transfers between devices, per_device(): lax.psum_scatter(rows_product(e_cone, g_two) + rows_product(h_one, e_atwo...  73.3 us
    all_gather x1, waiting for transfers between devices, per_device(): lax.all_gather(w_second, 'blk', axis=0, tiled=True)  41 us
    all_gather x1, waiting for transfers between devices, per_device(): lax.all_gather(w_first, 'blk', axis=0, tiled=True)  39.5 us
    psum x1, blocking collectives, per_device(): grad_out = lax.psum(grad_three, 'blk')  31.6 us
    unnamed x5, waiting for transfers between devices  22.9 us
    dot_general x4, matrix products, rows_product(): lax.dot_general(left, right, (((0,), (0,)), ((), ())), preferred_element_...  8.39 us
    unnamed x28, local copies, waits for them, and re-layouts  6.99 us
  transfers between devices with their start and end apart: 4, of which 4 were waited for; matrix products, arithmetic and copies ran while one was open for 4% of the time, Pallas kernels for 0%

commit v1 on v0

--- a/solution.py
+++ b/solution.py
@@ -2,6 +2,28 @@
 import jax.numpy as jnp
 from jax import lax
 from jax.sharding import PartitionSpec as P
+
+
+def joined_along(blocks, dim):
+    lengths = list(blocks.shape[1:])
+    lengths[dim] *= blocks.shape[0]
+    return jnp.moveaxis(blocks, 0, dim).reshape(lengths)
+
+
+def gather_around(array, axis, dim):
+    size = lax.axis_size(axis)
+    pairs = [(i, (i + 1) % size) for i in range(size)]
+    back = [(b, a) for a, b in pairs]
+    lower, upper = ([], [])
+    for turn in range(size - 1):
+        if turn % 2 == 0:
+            lower.append(lax.ppermute(lower[-1] if lower else array, axis, pairs))
+        else:
+            upper.append(lax.ppermute(upper[-1] if upper else array, axis, back))
+    parts = jnp.stack([*lower[::-1], array, *upper])
+    shift = lax.axis_index(axis) - len(lower)
+    parts = parts[(jnp.arange(size) - shift) % size]
+    return joined_along(parts, dim)
 
 
 def rows_product(left, right):
@@ -55,7 +77,7 @@
     position = lax.axis_index("blk")
     rows_dev = paths.shape[0]
     w_one, w_two = (
-        lax.all_gather(w_first, "blk", axis=0, tiled=True),
+        gather_around(w_first, "blk", 0),
         lax.all_gather(w_second, "blk", axis=0, tiled=True),
     )
     sending = lax.dynamic_index_in_dim(counts, position, 0, keepdims=False)

time: 255 us -> 241 us (0.945)
  waiting for transfers between devices: 177 us -> 129 us
  starting transfers between devices: 0.16 us -> 31.8 us
    all_gather x1 -> x0, waiting for transfers between devices: 39.5 us -> none  [per_device(): lax.all_gather(w_first, 'blk', axis=0, tiled=True)]
    ppermute x0 -> x15, starting transfers between devices: none -> 31.7 us  [the longest x7 31.2 us: gather_around(): upper.append(lax.ppermute(upper[-1] if upper else array, axis, back))]
    all_gather x1, waiting for transfers between devices: 41 us -> 13.5 us  [per_device(): lax.all_gather(w_second, 'blk', axis=0, tiled=True)]
    ppermute x0 -> x15, waiting for transfers between devices: none -> 20.3 us  [the longest x8 15.8 us: gather_around(): lower.append(lax.ppermute(lower[-1] if lower else array, axis, pairs))]
    unnamed x5 -> x4, waiting for transfers between devices: 22.9 us -> 21.2 us
    unnamed x28 -> x41, local copies, waits for them, and re-layouts: 6.99 us -> 7.91 us
  transfers between devices with their start and end apart: 4 -> 18, of which waited for: 4 -> 16; matrix products, arithmetic and copies ran while one was open for 4% -> 5% of each run, Pallas kernels for 0% -> 0%
where the time goes in v1:
time: 241 us; the launch traced here: 240 us
  waiting for transfers between devices  129 us (54%)
  blocking collectives  32.2 us (13%)
  starting transfers between devices  31.8 us (13%)
  matrix products  16.7 us (7%)
  between operations  14.7 us (6%)
  local copies, waits for them, and re-layouts  8.53 us (4%)
  other arithmetic  7.63 us (3%)
    reduce_scatter x1, waiting for transfers between devices, per_device(): lax.psum_scatter(rows_product(e_cone, g_two) + rows_product(h_one, e_atwo...  73.6 us
    psum x1, blocking collectives, per_device(): grad_out = lax.psum(grad_three, 'blk')  32.2 us
    ppermute x7, starting transfers between devices, gather_around(): upper.append(lax.ppermute(upper[-1] if upper else array, axis, back))  31.2 us
    unnamed x4, waiting for transfers between devices  21.2 us
    ppermute x8, waiting for transfers between devices, gather_around(): lower.append(lax.ppermute(lower[-1] if lower else array, axis, pairs))  15.8 us
    all_gather x1, waiting for transfers between devices, per_device(): lax.all_gather(w_second, 'blk', axis=0, tiled=True)  13.5 us
    dot_general x4, matrix products, rows_product(): lax.dot_general(left, right, (((0,), (0,)), ((), ())), preferred_element_...  8.48 us
    unnamed x41, local copies, waits for them, and re-layouts  7.91 us
  transfers between devices with their start and end apart: 18, of which 16 were waited for; matrix products, arithmetic and copies ran while one was open for 5% of the time, Pallas kernels for 0%

profile of v1, /device:TPU:0, one launch (start us, length us, event | category | flops | bytes accessed | tf_op | source)
XLA Modules:
  0.0 240.2 jit_solution(3157014332496207057)
XLA Ops:
  7.2 0.0 copy-start
  7.2 0.0 all-gather.2.cloned.1.call-start
  7.2 0.5 collective-permute-start
  7.7 7.2 %collective-permute-done = bf16[32,1024]{1,0:T(8,128)(2,1)S(1)} collective-permute-done((bf16[32,1024]{1,0:T(8,128)(2,1)}, bf16[32,1024]{1,0:T(8,128)(2,1)S(1)}, u32[]{:S(2)}, u32[]{:S(2)}) %collective-permute-start) | collective-permute-done | bytes 65568 | tf_op jit(solution)/shard_map/ppermute | solution.py:20
  14.9 0.0 collective-permute-start.1
  14.9 4.4 %collective-permute-start.8 = (bf16[32,1024]{1,0:T(8,128)(2,1)}, bf16[32,1024]{1,0:T(8,128)(2,1)S(1)}, u32[]{:S(2)}, u32[]{:S(2)}) collective-permute-start(bf16[32,1024]{1,0:T(8,128)(2,1)} %param.14), channel_id=1, source_target_pairs={{1,0},{2,1},{3,2},{4,3},{5,4},{6,5},{7,6},{8,7},{9,8},{10,9},{11,1... | collective-permute-start | bytes 196616 | tf_op jit(solution)/shard_map/ppermute | solution.py:22
  19.3 1.9 collective-permute-done.1
  21.3 0.0 collective-permute-start.2
  21.3 0.3 collective-permute-done.8
  21.6 4.4 %collective-permute-start.9 = (bf16[32,1024]{1,0:T(8,128)(2,1)S(1)}, bf16[32,1024]{1,0:T(8,128)(2,1)S(1)}, u32[]{:S(2)}, u32[]{:S(2)}) collective-permute-start(bf16[32,1024]{1,0:T(8,128)(2,1)S(1)} %collective-permute-done.8), channel_id=1, source_target_pairs={{1,0},{2,1},{3,2},{4,3},{5,4},{6,5},{7,6},{8,7},{9,8},{10,9},{11,1... | collective-permute-start | bytes 196616 | tf_op jit(solution)/shard_map/ppermute | solution.py:22
  25.9 1.7 collective-permute-done.2
  27.7 0.2 collective-permute-done.9
  27.8 4.5 %collective-permute-start.10 = (bf16[32,1024]{1,0:T(8,128)(2,1)S(1)}, bf16[32,1024]{1,0:T(8,128)(2,1)S(1)}, u32[]{:S(2)}, u32[]{:S(2)}) collective-permute-start(bf16[32,1024]{1,0:T(8,128)(2,1)S(1)} %collective-permute-done.9), channel_id=1, source_target_pairs={{1,0},{2,1},{3,2},{4,3},{5,4},{6,5},{7,6},{8,7},{9,8},{10,9},{11,1... | collective-permute-start | bytes 196616 | tf_op jit(solution)/shard_map/ppermute | solution.py:22
  32.3 1.8 collective-permute-done.3
  34.1 0.0 all-gather.2.cloned.1.call-update
  34.1 0.0 reduce-scatter.7.cloned.1.call-start
  34.2 1.3 dynamic-slice_reduce_fusion
  35.5 4.4 %collective-permute-start.11 = (bf16[32,1024]{1,0:T(8,128)(2,1)S(1)}, bf16[32,1024]{1,0:T(8,128)(2,1)S(1)}, u32[]{:S(2)}, u32[]{:S(2)}) collective-permute-start(bf16[32,1024]{1,0:T(8,128)(2,1)S(1)} %collective-permute-done.10), channel_id=1, source_target_pairs={{1,0},{2,1},{3,2},{4,3},{5,4},{6,5},{7,6},{8,7},{9,8},{10,9},{11,1... | collective-permute-start | bytes 196616 | tf_op jit(solution)/shard_map/ppermute | solution.py:22
  40.0 0.6 collective-permute-done.4
  40.5 1.3 collective-permute-done.11
  41.9 4.5 %collective-permute-start.12 = (bf16[32,1024]{1,0:T(8,128)(2,1)S(1)}, bf16[32,1024]{1,0:T(8,128)(2,1)S(1)}, u32[]{:S(2)}, u32[]{:S(2)}) collective-permute-start(bf16[32,1024]{1,0:T(8,128)(2,1)S(1)} %collective-permute-done.11), channel_id=1, source_target_pairs={{1,0},{2,1},{3,2},{4,3},{5,4},{6,5},{7,6},{8,7},{9,8},{10,9},{11,1... | collective-permute-start | bytes 196616 | tf_op jit(solution)/shard_map/ppermute | solution.py:22
  46.3 0.6 collective-permute-done.5
  47.0 1.3 collective-permute-done.12
  48.3 4.5 %collective-permute-start.13 = (bf16[32,1024]{1,0:T(8,128)(2,1)S(1)}, bf16[32,1024]{1,0:T(8,128)(2,1)S(1)}, u32[]{:S(2)}, u32[]{:S(2)}) collective-permute-start(bf16[32,1024]{1,0:T(8,128)(2,1)S(1)} %collective-permute-done.12), channel_id=1, source_target_pairs={{1,0},{2,1},{3,2},{4,3},{5,4},{6,5},{7,6},{8,7},{9,8},{10,9},{11,1... | collective-permute-start | bytes 196616 | tf_op jit(solution)/shard_map/ppermute | solution.py:22
  52.8 1.4 collective-permute-done.6
  54.2 0.6 compare_select_fusion.5
  54.8 0.7 convert_element_type.33
  55.5 4.4 %collective-permute-start.14 = (bf16[32,1024]{1,0:T(8,128)(2,1)S(1)}, bf16[32,1024]{1,0:T(8,128)(2,1)S(1)}, u32[]{:S(2)}, u32[]{:S(2)}) collective-permute-start(bf16[32,1024]{1,0:T(8,128)(2,1)S(1)} %collective-permute-done.13), channel_id=1, source_target_pairs={{1,0},{2,1},{3,2},{4,3},{5,4},{6,5},{7,6},{8,7},{9,8},{10,9},{11,1... | collective-permute-start | bytes 196616 | tf_op jit(solution)/shard_map/ppermute | solution.py:22
  60.0 0.6 collective-permute-done.7
  60.7 0.9 bitcast_dynamic-update-slice_fusion.7
  61.6 1.5 collective-permute-done.14
  63.1 0.6 gather_fusion
  63.7 0.5 convolution_bitcast_fusion
  64.2 13.5 %all-gather.2.cloned.1.call-done = bf16[1024,1024]{1,0:T(8,128)(2,1)} async-done(((bf16[64,1024]{1,0:T(8,128)(2,1)}), bf16[1024,1024]{1,0:T(8,128)(2,1)}) %all-gather.2.cloned.1.call-update) | async-done | bytes 2097168 | tf_op jit(solution)/shard_map/all_gather | solution.py:81
  77.7 2.9 %multiply_reduce_fusion.1 = (f32[128]{0:T(128)S(1)}, f32[128,1024]{0,1:T(8,128)S(1)}) fusion(f32[1024]{0:T(1024)S(1)} %convert_element_type.33, bf16[1024,1024]{1,0:T(8,128)(2,1)} %all-gather.2.cloned.1.call-done, f32[128,1024]{0,1:T(8,128)S(1)} %convolution_bitcast_fusion), kind=kOutput, calls=%fused_computation.18 | convolution fusion | flops 270401408 | bytes 3150336 | tf_op jit(solution)/shard_map/dot_general | solution.py:40
  80.6 0.0 copy-start.7
  80.7 1.6 multiply_convert_fusion.1
  82.3 0.5 fusion.4
  82.8 1.4 multiply_convert_fusion
  84.2 0.6 subtract_multiply_fusion
  84.8 1.4 add_reduce_fusion
  86.2 3.2 %fusion.2 = f32[1024,512]{1,0:T(8,128)S(1)} fusion(bf16[128,512]{1,0:T(8,128)(2,1)S(1)} %copy-done, bf16[1024,1024]{1,0:T(8,128)(2,1)} %all-gather.2.cloned.1.call-done, bf16[128,1024]{0,1:T(8,128)(2,1)S(1)} %get-tuple-element.10, f32[128,1024]{0,1:T(8,128)} %get-tuple-element.14, f32[128,1024]{0,1:T(8,128)} %get-tuple-element.12, ...), kind=kOutput, calls=%fused_computation.9 | convolution fusion | flops 403963904 | bytes 6160384 | tf_op jit(solution)/shard_map/dot_general | solution.py:30
  89.4 1.7 bitcast_add_fusion
  91.1 2.9 %copy.48 = f32[512,1024]{1,0:T(8,128)} copy(f32[512,1024]{0,1:T(8,128)} %bitcast_add_fusion) | data formatting | bytes 4194304
  94.0 0.0 reduce-scatter.7.cloned.1.call-update
  94.1 0.0 reduce-scatter.5.cloned.1.call-start
  94.1 1.0 copy-done.3
  95.1 0.1 copy-done.5
  95.1 0.8 fusion.17
  96.0 2.7 %convolution_add_fusion = f32[1024,1024]{1,0:T(8,128)} fusion(f32[1024,1024]{1,0:T(8,128)S(1)} %fusion.17, bf16[128,1024]{0,1:T(8,128)(2,1)S(1)} %get-tuple-element.10, f32[128,1024]{0,1:T(8,128)S(1)} %convolution_bitcast_fusion), kind=kOutput, calls=%fused_computation.1 | convolution fusion | flops 270401536 | bytes 9175040 | tf_op jit(solution)/shard_map/dot_general | solution.py:30
  98.7 0.0 reduce-scatter.5.cloned.1.call-update
  98.7 0.9 copy-done.8
  99.6 0.2 copy.28
  99.8 32.2 %psum.7 = f32[1024]{0:T(1024)S(1)} all-reduce(f32[1024]{0:T(1024)S(1)} %get-tuple-element.9), channel_id=1, replica_groups=mesh['groups'=2,'blk'=16] {'blk'}, use_global_device_ids=true, to_apply=%region_7.8 | all-reduce | flops 1024 | bytes 8192 | tf_op jit(solution)/shard_map/psum | solution.py:102
  132.0 0.6 multiply_reduce_fusion.3
  133.3 0.6 multiply_add_fusion.2
  133.9 21.1 %reduce-scatter.7.cloned.1.call-done = f32[32,1024]{1,0:T(8,128)} async-done(((f32[512,1024]{1,0:T(8,128)}), f32[32,1024]{1,0:T(8,128)}) %reduce-scatter.7.cloned.1.call-update) | async-done | bytes 131088
  155.0 1.1 copy.49
  156.1 0.2 multiply_reduce_fusion
  156.3 0.1 multiply_add_fusion
  156.4 0.8 copy.42
  157.2 73.6 %reduce-scatter.5.cloned.1.call-done = f32[64,1024]{1,0:T(8,128)} async-done(((f32[1024,1024]{1,0:T(8,128)}), f32[64,1024]{1,0:T(8,128)}) %reduce-scatter.5.cloned.1.call-update) | async-done | bytes 262160 | tf_op jit(solution)/shard_map/reduce_scatter | solution.py:96
  230.8 1.1 multiply_reduce_fusion.2
  231.9 1.8 multiply_add_fusion.1
  (43 shorter events, 0.2 us)
Async XLA Ops:
  7.2 56.6 %copy-start = (bf16[128,512]{1,0:T(8,128)(2,1)S(1)}, bf16[128,512]{1,0:T(8,128)(2,1)}, u32[]{:S(2)}) copy-start(bf16[128,512]{1,0:T(8,128)(2,1)} %param.10) | copy-start | bytes 393220
  7.2 70.5 %all-gather.2.cloned.1.call-start = ((), (), s32[]{:S(2)}) async-start(), calls=%async_computation.2 | async-start | bytes 2228224 | tf_op jit(solution)/shard_map/all_gather | solution.py:81
  7.2 7.7 %collective-permute-start = (bf16[32,1024]{1,0:T(8,128)(2,1)}, bf16[32,1024]{1,0:T(8,128)(2,1)S(1)}, u32[]{:S(2)}, u32[]{:S(2)}) collective-permute-start(bf16[32,1024]{1,0:T(8,128)(2,1)} %param.14), channel_id=1, source_target_pairs={{0,1},{1,2},{2,3},{3,4},{4,5},{5,6},{6,7},{7,8},{8,9},{9,10},{10,1... | collective-permute-start | bytes 196616 | tf_op jit(solution)/shard_map/ppermute | solution.py:20
  14.9 6.4 %collective-permute-start.1 = (bf16[32,1024]{1,0:T(8,128)(2,1)S(1)}, bf16[32,1024]{1,0:T(8,128)(2,1)S(1)}, u32[]{:S(2)}, u32[]{:S(2)}) collective-permute-start(bf16[32,1024]{1,0:T(8,128)(2,1)S(1)} %collective-permute-done), channel_id=1, source_target_pairs={{0,1},{1,2},{2,3},{3,4},{4,5},{5,6},{6,7},{7,8},{8,9},{9,10},{10,1... | collective-permute-start | bytes 196616 | tf_op jit(solution)/shard_map/ppermute | solution.py:20
  14.9 6.7 %collective-permute-start.8 = (bf16[32,1024]{1,0:T(8,128)(2,1)}, bf16[32,1024]{1,0:T(8,128)(2,1)S(1)}, u32[]{:S(2)}, u32[]{:S(2)}) collective-permute-start(bf16[32,1024]{1,0:T(8,128)(2,1)} %param.14), channel_id=1, source_target_pairs={{1,0},{2,1},{3,2},{4,3},{5,4},{6,5},{7,6},{8,7},{9,8},{10,9},{11,1... | collective-permute-start | bytes 196616 | tf_op jit(solution)/shard_map/ppermute | solution.py:22
  21.3 6.4 %collective-permute-start.2 = (bf16[32,1024]{1,0:T(8,128)(2,1)S(1)}, bf16[32,1024]{1,0:T(8,128)(2,1)S(1)}, u32[]{:S(2)}, u32[]{:S(2)}) collective-permute-start(bf16[32,1024]{1,0:T(8,128)(2,1)S(1)} %collective-permute-done.1), channel_id=1, source_target_pairs={{0,1},{1,2},{2,3},{3,4},{4,5},{5,6},{6,7},{7,8},{8,9},{9,10},{10,1... | collective-permute-start | bytes 196616 | tf_op jit(solution)/shard_map/ppermute | solution.py:20
  21.6 6.3 %collective-permute-start.9 = (bf16[32,1024]{1,0:T(8,128)(2,1)S(1)}, bf16[32,1024]{1,0:T(8,128)(2,1)S(1)}, u32[]{:S(2)}, u32[]{:S(2)}) collective-permute-start(bf16[32,1024]{1,0:T(8,128)(2,1)S(1)} %collective-permute-done.8), channel_id=1, source_target_pairs={{1,0},{2,1},{3,2},{4,3},{5,4},{6,5},{7,6},{8,7},{9,8},{10,9},{11,1... | collective-permute-start | bytes 196616 | tf_op jit(solution)/shard_map/ppermute | solution.py:22
  27.7 6.4 %collective-permute-start.3 = (bf16[32,1024]{1,0:T(8,128)(2,1)S(1)}, bf16[32,1024]{1,0:T(8,128)(2,1)S(1)}, u32[]{:S(2)}, u32[]{:S(2)}) collective-permute-start(bf16[32,1024]{1,0:T(8,128)(2,1)S(1)} %collective-permute-done.2), channel_id=1, source_target_pairs={{0,1},{1,2},{2,3},{3,4},{4,5},{5,6},{6,7},{7,8},{8,9},{9,10},{10,1... | collective-permute-start | bytes 196616 | tf_op jit(solution)/shard_map/ppermute | solution.py:20
  27.8 7.7 %collective-permute-start.10 = (bf16[32,1024]{1,0:T(8,128)(2,1)S(1)}, bf16[32,1024]{1,0:T(8,128)(2,1)S(1)}, u32[]{:S(2)}, u32[]{:S(2)}) collective-permute-start(bf16[32,1024]{1,0:T(8,128)(2,1)S(1)} %collective-permute-done.9), channel_id=1, source_target_pairs={{1,0},{2,1},{3,2},{4,3},{5,4},{6,5},{7,6},{8,7},{9,8},{10,9},{11,1... | collective-permute-start | bytes 196616 | tf_op jit(solution)/shard_map/ppermute | solution.py:22
  34.1 6.4 %collective-permute-start.4 = (bf16[32,1024]{1,0:T(8,128)(2,1)S(1)}, bf16[32,1024]{1,0:T(8,128)(2,1)S(1)}, u32[]{:S(2)}, u32[]{:S(2)}) collective-permute-start(bf16[32,1024]{1,0:T(8,128)(2,1)S(1)} %collective-permute-done.3), channel_id=1, source_target_pairs={{0,1},{1,2},{2,3},{3,4},{4,5},{5,6},{6,7},{7,8},{8,9},{9,10},{10,1... | collective-permute-start | bytes 196616 | tf_op jit(solution)/shard_map/ppermute | solution.py:20
  34.1 120.9 %reduce-scatter.7.cloned.1.call-start = ((), (), s32[]{:S(2)}) async-start(), calls=%async_computation.4 | async-start | bytes 2228224
  35.5 6.3 %collective-permute-start.11 = (bf16[32,1024]{1,0:T(8,128)(2,1)S(1)}, bf16[32,1024]{1,0:T(8,128)(2,1)S(1)}, u32[]{:S(2)}, u32[]{:S(2)}) collective-permute-start(bf16[32,1024]{1,0:T(8,128)(2,1)S(1)} %collective-permute-done.10), channel_id=1, source_target_pairs={{1,0},{2,1},{3,2},{4,3},{5,4},{6,5},{7,6},{8,7},{9,8},{10,9},{11,1... | collective-permute-start | bytes 196616 | tf_op jit(solution)/shard_map/ppermute | solution.py:22
  40.5 6.4 %collective-permute-start.5 = (bf16[32,1024]{1,0:T(8,128)(2,1)S(1)}, bf16[32,1024]{1,0:T(8,128)(2,1)S(1)}, u32[]{:S(2)}, u32[]{:S(2)}) collective-permute-start(bf16[32,1024]{1,0:T(8,128)(2,1)S(1)} %collective-permute-done.4), channel_id=1, source_target_pairs={{0,1},{1,2},{2,3},{3,4},{4,5},{5,6},{6,7},{7,8},{8,9},{9,10},{10,1... | collective-permute-start | bytes 196616 | tf_op jit(solution)/shard_map/ppermute | solution.py:20
  41.9 6.4 %collective-permute-start.12 = (bf16[32,1024]{1,0:T(8,128)(2,1)S(1)}, bf16[32,1024]{1,0:T(8,128)(2,1)S(1)}, u32[]{:S(2)}, u32[]{:S(2)}) collective-permute-start(bf16[32,1024]{1,0:T(8,128)(2,1)S(1)} %collective-permute-done.11), channel_id=1, source_target_pairs={{1,0},{2,1},{3,2},{4,3},{5,4},{6,5},{7,6},{8,7},{9,8},{10,9},{11,1... | collective-permute-start | bytes 196616 | tf_op jit(solution)/shard_map/ppermute | solution.py:22
  47.0 7.2 %collective-permute-start.6 = (bf16[32,1024]{1,0:T(8,128)(2,1)S(1)}, bf16[32,1024]{1,0:T(8,128)(2,1)S(1)}, u32[]{:S(2)}, u32[]{:S(2)}) collective-permute-start(bf16[32,1024]{1,0:T(8,128)(2,1)S(1)} %collective-permute-done.5), channel_id=1, source_target_pairs={{0,1},{1,2},{2,3},{3,4},{4,5},{5,6},{6,7},{7,8},{8,9},{9,10},{10,1... | collective-permute-start | bytes 196616 | tf_op jit(solution)/shard_map/ppermute | solution.py:20
  48.3 7.3 %collective-permute-start.13 = (bf16[32,1024]{1,0:T(8,128)(2,1)S(1)}, bf16[32,1024]{1,0:T(8,128)(2,1)S(1)}, u32[]{:S(2)}, u32[]{:S(2)}) collective-permute-start(bf16[32,1024]{1,0:T(8,128)(2,1)S(1)} %collective-permute-done.12), channel_id=1, source_target_pairs={{1,0},{2,1},{3,2},{4,3},{5,4},{6,5},{7,6},{8,7},{9,8},{10,9},{11,1... | collective-permute-start | bytes 196616 | tf_op jit(solution)/shard_map/ppermute | solution.py:22
  54.2 6.4 %collective-permute-start.7 = (bf16[32,1024]{1,0:T(8,128)(2,1)S(1)}, bf16[32,1024]{1,0:T(8,128)(2,1)S(1)}, u32[]{:S(2)}, u32[]{:S(2)}) collective-permute-start(bf16[32,1024]{1,0:T(8,128)(2,1)S(1)} %collective-permute-done.6), channel_id=1, source_target_pairs={{0,1},{1,2},{2,3},{3,4},{4,5},{5,6},{6,7},{7,8},{8,9},{9,10},{10,1... | collective-permute-start | bytes 196616 | tf_op jit(solution)/shard_map/ppermute | solution.py:20
  55.5 7.6 %collective-permute-start.14 = (bf16[32,1024]{1,0:T(8,128)(2,1)S(1)}, bf16[32,1024]{1,0:T(8,128)(2,1)S(1)}, u32[]{:S(2)}, u32[]{:S(2)}) collective-permute-start(bf16[32,1024]{1,0:T(8,128)(2,1)S(1)} %collective-permute-done.13), channel_id=1, source_target_pairs={{1,0},{2,1},{3,2},{4,3},{5,4},{6,5},{7,6},{8,7},{9,8},{10,9},{11,1... | collective-permute-start | bytes 196616 | tf_op jit(solution)/shard_map/ppermute | solution.py:22
  77.7 2.9 %copy-start.1 = (bf16[1024,1024]{1,0:T(8,128)(2,1)S(1)}, bf16[1024,1024]{1,0:T(8,128)(2,1)}, u32[]{:S(2)}) copy-start(bf16[1024,1024]{1,0:T(8,128)(2,1)} %all-gather.2.cloned.1.call-done) | copy-start | bytes 6291460
  80.6 4.2 %copy-start.2 = (f32[128,1024]{0,1:T(8,128)}, f32[128,1024]{0,1:T(8,128)S(1)}, u32[]{:S(2)}) copy-start(f32[128,1024]{0,1:T(8,128)S(1)} %get-tuple-element.16) | copy-start | bytes 1572868
  80.6 1.6 copy-start.7
  82.3 1.9 copy-start.10
  84.2 2.0 copy-start.4
  94.0 1.0 copy-start.3
  94.0 1.1 copy-start.5
  94.1 136.8 %reduce-scatter.5.cloned.1.call-start = ((), (), s32[]{:S(2)}) async-start(), calls=%async_computation.3 | async-start | bytes 4456448 | tf_op jit(solution)/shard_map/reduce_scatter | solution.py:96
  98.7 0.9 copy-start.8
  98.7 34.6 %copy-start.9 = (f32[1024]{0:T(1024)S(1)}, f32[1024]{0:T(1024)}, u32[]{:S(2)}) copy-start(f32[1024]{0:T(1024)} %param.19) | copy-start | bytes 12292
  99.6 132.3 %copy-start.6 = (f32[64,1024]{1,0:T(8,128)S(1)}, f32[64,1024]{1,0:T(8,128)}, u32[]{:S(2)}) copy-start(f32[64,1024]{1,0:T(8,128)} %param.18) | copy-start | bytes 786436
Sparse Core Ops, SparseCore 0:
  34.3 43.4 all-gather.1
  94.2 60.7 reduce-scatter.6
  159.4 71.3 reduce-scatter.4
